TPU v7x, 512 devices: a whole 4x4x16 slice. The times are simulated.
512 devices in a mesh: seg: 64 (over y, z_lo, core), blk: 8 (over x, z_hi).
Axes of the slice: x: 4, y: 4, z: 16 (z_hi: 2, z_lo: 8; z = z_hi * 8 + z_lo), core: 2. Of those that a mesh axis runs over, the one named last changes fastest.
Arguments:
- record: float32 [24, 262144], P(None, ('seg', 'blk')), may hold values from -8 to 8, as said below
- templates: bfloat16 [128, 24, 512], P('blk'), may hold values from -6 to 6
Outputs:
- detection: float32 [128, 262144], P(None, ('seg', 'blk'))
Inputs may be any that keep to these rules, and one draw needn't show every extreme that they name: `record`: network samples.
All inputs are finite; a program needn't handle non-finite values.
Results may differ from a plain program's by a relative error of at most 0.0032.
Values may be sent and summed in bfloat16 or wider, within the bound.
No kernel may reach another device: no remote copies, remote signals or barrier semaphores. Data moves between devices by JAX's collectives and lax.ppermute only.
A program may use at most 64 MiB of HBM per device.

v0:
```python
import jax
import jax.numpy as jnp
from jax import lax
from jax.sharding import PartitionSpec as P


def passed_along(block, axis, distance):
    devices = range(lax.axis_size(axis))
    route = [(i - distance, i) for i in devices if i - distance in devices]
    return lax.ppermute(block, axis, route)


def normalize(templates):
    widened = templates.astype(jnp.float32)
    centred = widened - jnp.mean(widened, axis=2, keepdims=True)
    return (centred / jnp.sqrt(jnp.sum(centred * centred, axis=2, keepdims=True) + 1e-06)).astype(
        jnp.bfloat16
    )


def band_matrix(samples, window):
    span = samples + window - 1
    rows = jnp.arange(span, dtype=jnp.int32)[:, None]
    cols = jnp.arange(samples, dtype=jnp.int32)[None, :]
    inside = jnp.logical_and(rows >= cols, rows < cols + window)
    return inside.astype(jnp.float32)


def window_scale(extended, band, window):
    stacked_rows = jnp.concatenate([extended, extended * extended], axis=0)
    sums = jnp.dot(
        stacked_rows, band, precision=lax.Precision.HIGHEST, preferred_element_type=jnp.float32
    )
    channels = extended.shape[0]
    window_sum = sums[:channels]
    window_sq = sums[channels:]
    spread = window_sq - window_sum * window_sum / window
    return 1.0 / jnp.sqrt(jnp.maximum(spread, 1.0))


def correlate(record_bf, kernel_block, scale):
    members = kernel_block.shape[0]
    channels = kernel_block.shape[1]
    window = kernel_block.shape[2]
    samples = scale.shape[1]
    span = record_bf.shape[1]
    kernels = jnp.transpose(kernel_block, (1, 0, 2))

    def one_channel(total, inputs):
        channel_row, kernel_rows, factor = inputs
        repeated = jnp.tile(channel_row, window + 1)[: window * (span + 1)]
        hankel = repeated.reshape(window, span + 1)[:, :samples]
        product = jnp.dot(kernel_rows, hankel, preferred_element_type=jnp.float32)
        return (total + product * factor[None, :], None)

    total, unused = lax.scan(
        one_channel, jnp.zeros((members, samples), jnp.float32), (record_bf, kernels, scale)
    )
    return total / channels


def body(record, templates):
    samples = record.shape[1]
    window = templates.shape[2]
    trailing = passed_along(record, ("seg", "blk"), -1)
    padded_rec = jnp.concatenate([record, trailing], axis=1)
    normalized = normalize(templates)
    band = band_matrix(samples, window)
    extended = padded_rec[:, : samples + window - 1]
    scale = window_scale(extended, band, window)
    record_bf = extended.astype(jnp.bfloat16)
    collected = lax.all_gather(normalized, "blk", axis=0, tiled=True)
    stacked = correlate(record_bf, collected, scale)
    power_sum = lax.psum(jnp.sum(stacked * stacked, axis=1), ("seg", "blk"))
    record_len = samples * lax.axis_size("seg") * lax.axis_size("blk")
    return stacked / jnp.sqrt(power_sum / record_len + 1e-06)[:, None]


def solution(mesh):
    return jax.shard_map(
        body,
        mesh=mesh,
        in_specs=(P(None, ("seg", "blk")), P("blk", None, None)),
        out_specs=P(None, ("seg", "blk")),
        check_vma=False,
    )
```

profile of v0, /device:TPU:1, one launch (start us, length us, event | category | flops | bytes accessed | tf_op | source)
XLA Modules:
  0.0 357.7 jit_solution(17654023932856735463)
XLA Ops:
  6.5 1.2 convert_reduce_fusion
  7.7 1.3 fusion.11
  9.0 1.9 fusion.12
  11.0 19.0 %collective-permute-start = (f32[24,512]{1,0:T(8,128)}, f32[24,512]{1,0:T(8,128)S(1)}, u32[]{:S(2)}, u32[]{:S(2)}) collective-permute-start(f32[24,512]{1,0:T(8,128)} %param.4), channel_id=1, source_target_pairs={{1,0},{2,1},{3,2},{4,3},{5,4},{6,5},{7,6},{8,7},{9,8},{10,9},{11,1... | collective-permute-start | bytes 147464 | tf_op jit(solution)/shard_map/ppermute | solution.py:10
  30.0 1.5 collective-permute-done
  32.4 129.1 %all-gather.2.cloned.1.call-done = bf16[128,24,512]{2,0,1:T(8,128)(2,1)} async-done(((bf16[16,24,512]{2,0,1:T(8,128)(2,1)}), bf16[128,24,512]{2,0,1:T(8,128)(2,1)}) %all-gather.2.cloned.1.call-update) | async-done | bytes 3145744 | tf_op jit(solution)/shard_map/all_gather | solution.py:72
  161.6 86.4 %while.11 = (s32[]{:T(128)}, f32[128,512]{1,0:T(8,128)S(1)}, bf16[24,128,512]{2,1,0:T(8,128)(2,1)}, bf16[24,1023]{1,0:T(8,128)(2,1)S(1)}, f32[24,512]{1,0:T(8,128)S(1)}, /*index=5*/s32[]{:T(128)}, s32[]{:T(128)}) while((s32[]{:T(128)}, f32[128,512]{1,0:T(8,128)S(1)}, bf16[24,128,512]{2,1,0:T(8,128)(2,1)}, ...), condition=%wide.region_3.4_spmd.clone, body=%wide.region_2.3_spmd.clone.sunk | while | flops 67305472 | bytes 8535635 | solution.py:56
  161.7 1.6 tile.17
  164.0 1.2 fusion.28
  165.3 1.6 tile.17
  167.6 1.2 fusion.28
  168.9 1.6 tile.17
  171.2 1.2 fusion.28
  172.5 1.6 tile.17
  174.8 1.2 fusion.28
  176.1 1.6 tile.17
  178.3 1.2 fusion.28
  179.7 1.6 tile.17
  181.9 1.2 fusion.28
  183.3 1.6 tile.17
  185.5 1.2 fusion.28
  186.9 1.6 tile.17
  189.1 1.2 fusion.28
  190.5 1.6 tile.17
  192.7 1.2 fusion.28
  194.1 1.6 tile.17
  197.7 1.6 tile.17
  199.9 1.2 fusion.28
  201.3 1.6 tile.17
  204.9 1.6 tile.17
  207.1 1.2 fusion.28
  208.5 1.6 tile.17
  212.1 1.6 tile.17
  214.3 1.2 fusion.28
  215.7 1.6 tile.17
  219.3 1.6 tile.17
  221.5 1.2 fusion.28
  222.9 1.6 tile.17
  226.5 1.6 tile.17
  228.7 1.2 fusion.28
  230.1 1.6 tile.17
  233.7 1.6 tile.17
  235.9 1.2 fusion.28
  237.3 1.6 tile.17
  240.9 1.6 tile.17
  243.1 1.2 fusion.28
  244.5 1.6 tile.17
  248.1 102.0 %psum.7 = f32[128]{0:T(128)S(1)} all-reduce(f32[128]{0:T(128)S(1)} %multiply_reduce_fusion), channel_id=1, replica_groups=mesh['seg'=64,'blk'=8] {'seg','blk'}, use_global_device_ids=true, to_apply=%region_5.6 | all-reduce | flops 128 | bytes 1024 | tf_op jit(solution)/shard_map/psum | solution.py:74
  (143 shorter events, 28.6 us)
Async XLA Ops:
  6.5 25.0 %copy-start = (f32[24,512]{1,0:T(8,128)S(1)}, f32[24,512]{1,0:T(8,128)}, u32[]{:S(2)}) copy-start(f32[24,512]{1,0:T(8,128)} %param.4) | copy-start | bytes 147460
  6.5 155.0 %all-gather.2.cloned.1.call-start = ((), (), s32[]{:S(2)}) async-start(), calls=%async_computation | async-start | bytes 3538944 | tf_op jit(solution)/shard_map/all_gather | solution.py:72
  11.0 20.5 %collective-permute-start = (f32[24,512]{1,0:T(8,128)}, f32[24,512]{1,0:T(8,128)S(1)}, u32[]{:S(2)}, u32[]{:S(2)}) collective-permute-start(f32[24,512]{1,0:T(8,128)} %param.4), channel_id=1, source_target_pairs={{1,0},{2,1},{3,2},{4,3},{5,4},{6,5},{7,6},{8,7},{9,8},{10,9},{11,1... | collective-permute-start | bytes 147464 | tf_op jit(solution)/shard_map/ppermute | solution.py:10
Sparse Core Ops, SparseCore 0:
  11.1 150.3 all-gather.1
where the time goes:
time: 358 us
  waiting for transfers between devices  131 us (37%)
  blocking collectives  102 us (28%)
  local copies, waits for them, and re-layouts  56.6 us (16%)
  matrix products  29 us (8%)
  starting transfers between devices  19 us (5%)
  between operations  13.5 us (4%)
  other arithmetic  5.36 us (1%)
    all_gather x1, waiting for transfers between devices, body(): collected = lax.all_gather(normalized, 'blk', axis=0, tiled=True)  129 us
    psum x1, blocking collectives, body(): power_sum = lax.psum(jnp.sum(stacked * stacked, axis=1), ('seg', 'blk'))  102 us
    another operation x48, local copies, waits for them, and re-layouts, one_channel(): repeated = jnp.tile(channel_row, window + 1)[:window * (span + 1)]  42.1 us
    dot_general x24, matrix products, one_channel(): product = jnp.dot(kernel_rows, hankel, preferred_element_type=jnp.float32)  28.2 us
    ppermute x1, starting transfers between devices, passed_along(): return lax.ppermute(block, axis, route)  19 us
    reshape x24, local copies, waits for them, and re-layouts, one_channel(): hankel = repeated.reshape(window, span + 1)[:, :samples]  11.8 us
  transfers between devices with their start and end apart: 2, of which 2 were waited for; matrix products, arithmetic and copies ran while one was open for 0% of the time, Pallas kernels for 0%

commit v1 on v0

--- a/solution.py
+++ b/solution.py
@@ -69,7 +69,9 @@
     extended = padded_rec[:, : samples + window - 1]
     scale = window_scale(extended, band, window)
     record_bf = extended.astype(jnp.bfloat16)
-    collected = lax.all_gather(normalized, "blk", axis=0, tiled=True)
+    collected = jnp.concatenate(
+        lax.all_to_all(jnp.stack([normalized] * lax.axis_size("blk")), "blk", 0, 0), axis=0
+    )
     stacked = correlate(record_bf, collected, scale)
     power_sum = lax.psum(jnp.sum(stacked * stacked, axis=1), ("seg", "blk"))
     record_len = samples * lax.axis_size("seg") * lax.axis_size("blk")

time: 358 us -> 372 us (1.039)
  blocking collectives: 102 us -> 182 us
  waiting for transfers between devices: 131 us -> 55.2 us
  starting transfers between devices: 19 us -> 33.5 us
  between operations: 13.5 us -> 0.11 us
  local copies, waits for them, and re-layouts: 56.6 us -> 65.3 us
    all_gather x1 -> x0, waiting for transfers between devices: 129 us -> none  [body(): collected = lax.all_gather(normalized, 'blk', axis=0, tiled=True)]
    psum x1, blocking collectives: 102 us -> 182 us  [body(): power_sum = lax.psum(jnp.sum(stacked * stacked, axis=1), ('seg', 'blk'))]
    ppermute x1, waiting for transfers between devices: 1.45 us -> 53.6 us  [passed_along(): return lax.ppermute(block, axis, route)]
    all_to_all x0 -> x1, starting transfers between devices: none -> 18.2 us  [body(): lax.all_to_all(jnp.stack([normalized] * lax.axis_size('blk')), 'blk', 0, 0)]
    all_to_all x0 -> x1, local copies, waits for them, and re-layouts: none -> 3.77 us  [body(): lax.all_to_all(jnp.stack([normalized] * lax.axis_size('blk')), 'blk', 0, 0)]
    ppermute x1, starting transfers between devices: 19 us -> 15.3 us  [passed_along(): return lax.ppermute(block, axis, route)]
where the time goes in v1:
time: 372 us; the launch traced here: 371 us
  blocking collectives  182 us (49%)
  local copies, waits for them, and re-layouts  65.3 us (18%)
  waiting for transfers between devices  55.2 us (15%)
  starting transfers between devices  33.5 us (9%)
  matrix products  29 us (8%)
  other arithmetic  4.51 us (1%)
    psum x1, blocking collectives, body(): power_sum = lax.psum(jnp.sum(stacked * stacked, axis=1), ('seg', 'blk'))  182 us
    ppermute x1, waiting for transfers between devices, passed_along(): return lax.ppermute(block, axis, route)  53.6 us
    another operation x48, local copies, waits for them, and re-layouts, one_channel(): repeated = jnp.tile(channel_row, window + 1)[:window * (span + 1)]  42.1 us
    dot_general x24, matrix products, one_channel(): product = jnp.dot(kernel_rows, hankel, preferred_element_type=jnp.float32)  28.2 us
    all_to_all x1, starting transfers between devices, body(): lax.all_to_all(jnp.stack([normalized] * lax.axis_size('blk')), 'blk', 0, 0)  18.2 us
    ppermute x1, starting transfers between devices, passed_along(): return lax.ppermute(block, axis, route)  15.3 us
    reshape x24, local copies, waits for them, and re-layouts, one_channel(): hankel = repeated.reshape(window, span + 1)[:, :samples]  11.8 us
  transfers between devices with their start and end apart: 2, of which 2 were waited for; matrix products, arithmetic and copies ran while one was open for 0% of the time, Pallas kernels for 0%

profile of v1, /device:TPU:1, one launch (start us, length us, event | category | flops | bytes accessed | tf_op | source)
XLA Modules:
  0.0 371.0 jit_solution(13646311777862588413)
XLA Ops:
  1.1 1.2 fusion.11
  2.4 1.2 fusion.12
  3.7 2.1 stack.2
  5.8 18.2 %all-to-all-start = ((bf16[8,16,24,512]{3,1,2,0:T(8,128)(2,1)}), bf16[8,16,24,512]{3,1,2,0:T(8,128)(2,1)}, u32[]{:S(2)}, u32[]{:S(2)}) async-start(bf16[8,16,24,512]{3,1,2,0:T(8,128)(2,1)} %stack.2), calls=%async_computation | async-start | bytes 6291456 | tf_op jit(solution)/shard_map/all_to_all | solution.py:73
  24.1 15.3 %collective-permute-start = (f32[24,512]{1,0:T(8,128)S(1)}, f32[24,512]{1,0:T(8,128)S(1)}, u32[]{:S(2)}, u32[]{:S(2)}) collective-permute-start(f32[24,512]{1,0:T(8,128)S(1)} %copy-done), channel_id=1, source_target_pairs={{1,0},{2,1},{3,2},{4,3},{5,4},{6,5},{7,6},{8,7},{9,8},{10,9},{11,1... | collective-permute-start | bytes 147464 | tf_op jit(solution)/shard_map/ppermute | solution.py:10
  39.4 53.6 %collective-permute-done = f32[24,512]{1,0:T(8,128)S(1)} collective-permute-done((f32[24,512]{1,0:T(8,128)S(1)}, f32[24,512]{1,0:T(8,128)S(1)}, u32[]{:S(2)}, u32[]{:S(2)}) %collective-permute-start) | collective-permute-done | bytes 49184 | tf_op jit(solution)/shard_map/ppermute | solution.py:10
  93.9 1.6 all-to-all-done
  95.5 3.8 %copy.6 = bf16[8,16,24,512]{3,2,1,0:T(8,128)(2,1)S(1)} copy(bf16[8,16,24,512]{3,1,2,0:T(8,128)(2,1)} %all-to-all-done) | data formatting | bytes 6291456 | tf_op jit(solution)/shard_map/all_to_all | solution.py:73
  99.3 2.7 copy.7
  102.0 86.4 %while.11 = (s32[]{:T(128)}, f32[128,512]{1,0:T(8,128)S(1)}, bf16[24,128,512]{2,1,0:T(8,128)(2,1)}, bf16[24,1023]{1,0:T(8,128)(2,1)S(1)}, f32[24,512]{1,0:T(8,128)S(1)}, /*index=5*/s32[]{:T(128)}, s32[]{:T(128)}) while((s32[]{:T(128)}, f32[128,512]{1,0:T(8,128)S(1)}, bf16[24,128,512]{2,1,0:T(8,128)(2,1)}, ...), condition=%wide.region_3.4_spmd.clone, body=%wide.region_2.3_spmd.clone.sunk | while | flops 67305472 | bytes 8535635 | solution.py:56
  102.2 1.6 tile.17
  104.4 1.2 fusion.28
  105.8 1.6 tile.17
  108.0 1.2 fusion.28
  109.4 1.6 tile.17
  111.6 1.2 fusion.28
  113.0 1.6 tile.17
  116.6 1.6 tile.17
  118.8 1.2 fusion.28
  120.2 1.6 tile.17
  123.8 1.6 tile.17
  126.0 1.2 fusion.28
  127.4 1.6 tile.17
  131.0 1.6 tile.17
  133.2 1.2 fusion.28
  134.6 1.6 tile.17
  138.2 1.6 tile.17
  140.4 1.2 fusion.28
  141.8 1.6 tile.17
  145.4 1.6 tile.17
  147.6 1.2 fusion.28
  149.0 1.6 tile.17
  152.6 1.6 tile.17
  154.8 1.2 fusion.28
  156.2 1.6 tile.17
  159.8 1.6 tile.17
  162.0 1.2 fusion.28
  163.4 1.6 tile.17
  167.0 1.6 tile.17
  169.2 1.2 fusion.28
  170.6 1.6 tile.17
  174.2 1.6 tile.17
  176.4 1.2 fusion.28
  177.8 1.6 tile.17
  181.4 1.6 tile.17
  183.6 1.2 fusion.28
  185.0 1.6 tile.17
  188.5 181.7 %psum.7 = f32[128]{0:T(128)S(1)} all-reduce(f32[128]{0:T(128)S(1)} %multiply_reduce_fusion), channel_id=1, replica_groups=mesh['seg'=64,'blk'=8] {'seg','blk'}, use_global_device_ids=true, to_apply=%region_5.6 | all-reduce | flops 128 | bytes 1024 | tf_op jit(solution)/shard_map/psum | solution.py:76
  (146 shorter events, 33.4 us)
Async XLA Ops:
  5.8 18.2 %copy-start = (f32[24,512]{1,0:T(8,128)S(1)}, f32[24,512]{1,0:T(8,128)}, u32[]{:S(2)}) copy-start(f32[24,512]{1,0:T(8,128)} %param.4) | copy-start | bytes 147460
  5.8 89.7 %all-to-all-start = ((bf16[8,16,24,512]{3,1,2,0:T(8,128)(2,1)}), bf16[8,16,24,512]{3,1,2,0:T(8,128)(2,1)}, u32[]{:S(2)}, u32[]{:S(2)}) async-start(bf16[8,16,24,512]{3,1,2,0:T(8,128)(2,1)} %stack.2), calls=%async_computation | async-start | bytes 6291456 | tf_op jit(solution)/shard_map/all_to_all | solution.py:73
  24.1 69.0 %collective-permute-start = (f32[24,512]{1,0:T(8,128)S(1)}, f32[24,512]{1,0:T(8,128)S(1)}, u32[]{:S(2)}, u32[]{:S(2)}) collective-permute-start(f32[24,512]{1,0:T(8,128)S(1)} %copy-done), channel_id=1, source_target_pairs={{1,0},{2,1},{3,2},{4,3},{5,4},{6,5},{7,6},{8,7},{9,8},{10,9},{11,1... | collective-permute-start | bytes 147464 | tf_op jit(solution)/shard_map/ppermute | solution.py:10
